TPU v7x, 128 devices: a whole 4x4x4 slice. The times are simulated.
128 devices in a mesh: pipe: 8 (over z, core), ctx: 16 (over y, x).
Axes of the slice: x: 4, y: 4, z: 4, core: 2. Of those that a mesh axis runs over, the one named last changes fastest.
Arguments:
- grad_in: bfloat16 [8, 4096, 8192], P('pipe', 'ctx'), may hold values from -6 to 6
- query: bfloat16 [8, 4096, 512], P('pipe', 'ctx'), may hold values from -8 to 8
- keyval: bfloat16 [8, 4096, 256], P('pipe', 'ctx'), may hold values from -8 to 8
- w_qkv: bfloat16 [8, 8192, 768], P('pipe', 'ctx'), may hold values from -0.0625 to 0.0625
- w_out: bfloat16 [8, 8192, 512], P('pipe', 'ctx'), may hold values from -0.25 to 0.25
- doc_lengths: int32 [8, 8], P('pipe'), may hold values from 1 to 2048, 4096 in all within a row
- order: int32 [8, 32], P('pipe'), may hold values from 0 to 31, as said below
Outputs:
- passed_grad: bfloat16 [8, 4096, 8192], P('pipe', 'ctx')
Inputs may be any that keep to these rules, and one draw needn't show every extreme that they name: Each row of order is a permutation of 0 to 31; entry d * 2 + k (device d's stored slot k, k < 2) names one of the sequence blocks e * 2 to e * 2 + 1 of device e = (d + k * 8) mod 16. `doc_lengths`: each row sums to 4096 and its largest entry is 2048.
All inputs are finite; a program needn't handle non-finite values.
Results may differ from a plain program's by a relative error of at most 0.015.
Values may be sent and summed in bfloat16 or wider, within the bound.
No kernel may reach another device: no remote copies, remote signals or barrier semaphores. Data moves between devices by JAX's collectives and lax.ppermute only.
A program may use at most 128 MiB of HBM per device.

v0:
```python
import math
import jax
import jax.numpy as jnp
from jax import lax
from jax.sharding import PartitionSpec as P

BLOCK = 128
ROPE_BASE = 500000.0
MASKED = -1e30


def passed_along(value, axis, steps):
    count = lax.axis_size(axis)
    pairs = [(source, (source + steps) % count) for source in range(count)]
    return lax.ppermute(value, axis, pairs)


def passed_along_2(value, axis, by):
    size = lax.axis_size(axis)
    pairs = [(i, i + by) for i in range(size) if 0 <= i + by < size]
    return lax.ppermute(value, axis, pairs)


def rope_tables(positions, head_dim):
    half_width = head_dim // 2
    inv_freq = ROPE_BASE ** (-(jnp.arange(half_width, dtype=jnp.float32) * 2.0 / head_dim))
    angles = positions.astype(jnp.float32)[:, None] * inv_freq[None, :]
    angles = jnp.concatenate([angles, angles], axis=1)
    return (jnp.cos(angles), jnp.sin(angles))


def unrotate(gradient, positions):
    cosine, sine_table = rope_tables(positions, gradient.shape[1])
    half_width = gradient.shape[1] // 2
    turned = jnp.concatenate([-gradient[:, half_width:], gradient[:, :half_width]], axis=1)
    return gradient * cosine - turned * sine_table


def doc_ids(positions, lengths):
    doc_ends = jnp.cumsum(lengths)[:-1]
    return jnp.sum((positions[:, None] >= doc_ends[None, :]).astype(jnp.int32), axis=1)


def seq_to_stored(rows, block_order, device, ctx_size, per_device):
    width = rows.shape[1]
    first_block = device * per_device
    blocks = rows.reshape(per_device, BLOCK, width)
    pieces = []
    for slot_k in range(per_device):
        offset = slot_k * ctx_size // per_device
        slot_at = (device - offset) % ctx_size * per_device + slot_k
        local_index = block_order[slot_at] - first_block
        chosen = lax.dynamic_index_in_dim(blocks, local_index, 0, keepdims=False)
        if slot_k > 0:
            chosen = passed_along(chosen, "ctx", -offset)
        pieces.append(chosen)
    return jnp.concatenate(pieces, axis=0)


def stored_to_seq(rows, block_order, device, ctx_size, per_device):
    width = rows.shape[1]
    first_block = device * per_device
    blocks = rows.reshape(per_device, BLOCK, width)
    pieces = []
    local_ids = []
    for slot_k in range(per_device):
        offset = slot_k * ctx_size // per_device
        piece = blocks[slot_k]
        if slot_k > 0:
            piece = passed_along(piece, "ctx", offset)
        pieces.append(piece)
        sender_slot = (device - offset) % ctx_size * per_device + slot_k
        local_ids.append(block_order[sender_slot] - first_block)
    stacked = jnp.stack(pieces)
    index_list = jnp.stack(local_ids)
    choose = (jnp.arange(per_device, dtype=jnp.int32)[:, None] == index_list[None, :]).astype(
        rows.dtype
    )
    placed = jnp.einsum("pk,kbw->pbw", choose, stacked, preferred_element_type=jnp.float32)
    return placed.astype(rows.dtype).reshape(-1, width)


def contract_rows(left_rows, right_rows):
    return lax.dot_general(
        left_rows, right_rows, (((0,), (0,)), ((), ())), preferred_element_type=jnp.float32
    )


def contract_cols(left_rows, right_rows):
    return lax.dot_general(
        left_rows, right_rows, (((1,), (1,)), ((), ())), preferred_element_type=jnp.float32
    )


def block_scores(query_rows, key_rows, query_pos, query_doc, key_pos, key_doc, score_scale):
    scores = contract_cols(query_rows, key_rows) * score_scale
    visible = (query_doc[:, None] == key_doc[None, :]) & (key_pos[None, :] <= query_pos[:, None])
    return (scores, visible)


def body(grad_in, query, keyval, w_qkv, w_out, doc_lengths, order):
    section_grad_in = grad_in[0]
    stored_query = query[0]
    stored_keyval = keyval[0]
    in_weight = w_qkv[0]
    out_weight = w_out[0]
    lengths = doc_lengths[0]
    block_order = order[0]
    ctx_size = lax.axis_size("ctx")
    device = lax.axis_index("ctx")
    local_rows = section_grad_in.shape[0]
    head_dim = stored_keyval.shape[1] // 2
    group = stored_query.shape[1] // head_dim
    per_device = local_rows // BLOCK
    block_count = block_order.shape[0]
    seq_len = local_rows * ctx_size
    first_row = device * local_rows
    score_scale = 1.0 / math.sqrt(head_dim)
    key_block = math.gcd(seq_len, 512)
    key_steps = seq_len // key_block
    within = jnp.arange(BLOCK, dtype=jnp.int32)
    out_grad = jnp.dot(
        section_grad_in,
        lax.all_gather(out_weight, "ctx", axis=0, tiled=True),
        preferred_element_type=jnp.float32,
    ).astype(jnp.bfloat16)
    local_out_grad = seq_to_stored(out_grad, block_order, device, ctx_size, per_device)
    query_positions = (block_order[:, None] * BLOCK + within[None, :]).reshape(-1)
    gathered = lax.all_gather(stored_keyval, "ctx", axis=0, tiled=True)
    slot_ids = jnp.arange(block_count, dtype=jnp.int32)
    inverse = jnp.sum(
        jnp.where(block_order[None, :] == slot_ids[:, None], slot_ids[None, :], 0), axis=1
    )
    all_keyval = gathered.reshape(block_count, BLOCK, 2 * head_dim)[inverse].reshape(
        seq_len, 2 * head_dim
    )
    key_positions = jnp.arange(seq_len, dtype=jnp.int32)
    key_docs = doc_ids(key_positions, lengths)
    query_pos = lax.dynamic_slice_in_dim(query_positions, first_row, local_rows)
    query_doc = doc_ids(query_pos, lengths)
    flat_rows = local_rows * group
    flat_query = stored_query.reshape(flat_rows, head_dim)
    flat_grad = local_out_grad.reshape(flat_rows, head_dim)
    flat_pos = jnp.repeat(query_pos, group)
    flat_doc = jnp.repeat(query_doc, group)
    key_blocks = (
        all_keyval.reshape(key_steps, key_block, 2 * head_dim),
        key_positions.reshape(key_steps, key_block),
        key_docs.reshape(key_steps, key_block),
    )

    def running_total(carried, current):
        row_top, row_total, weighted = carried
        pair_rows, key_pos, key_doc = current
        scores, visible = block_scores(
            flat_query, pair_rows[:, :head_dim], flat_pos, flat_doc, key_pos, key_doc, score_scale
        )
        new_top = jnp.maximum(row_top, jnp.max(jnp.where(visible, scores, MASKED), axis=1))
        rescale = jnp.exp(row_top - new_top)
        weights = jnp.where(visible, jnp.exp(scores - new_top[:, None]), 0.0)
        row_total = row_total * rescale + jnp.sum(weights, axis=1)
        value_wide = pair_rows[:, head_dim:].astype(jnp.float32)
        weighted = weighted * rescale[:, None] + jnp.dot(
            weights, value_wide, precision=lax.Precision.HIGHEST
        )
        return ((new_top, row_total, weighted), None)

    start_top = jnp.full((flat_rows,), MASKED, jnp.float32)
    start_carry = (
        start_top,
        jnp.zeros((flat_rows,), jnp.float32),
        jnp.zeros((flat_rows, head_dim), jnp.float32),
    )
    (row_top, row_total, weighted), unused = lax.scan(running_total, start_carry, key_blocks)
    log_total = row_top + jnp.log(row_total)
    attn_out = weighted / row_total[:, None]
    row_delta = jnp.sum(flat_grad.astype(jnp.float32) * attn_out, axis=1)

    def grad_step(summed, current):
        pair_rows, key_pos, key_doc = current
        scores, visible = block_scores(
            flat_query, pair_rows[:, :head_dim], flat_pos, flat_doc, key_pos, key_doc, score_scale
        )
        attn_prob = jnp.where(visible, jnp.exp(scores - log_total[:, None]), 0.0)
        prob_grad = contract_cols(flat_grad, pair_rows[:, head_dim:])
        score_grad = (score_scale * attn_prob * (prob_grad - row_delta[:, None])).astype(
            jnp.bfloat16
        )
        summed = summed + jnp.dot(
            score_grad, pair_rows[:, :head_dim], preferred_element_type=jnp.float32
        )
        key_term = contract_rows(score_grad, flat_query)
        value_term = contract_rows(attn_prob.astype(jnp.bfloat16), flat_grad)
        return (summed, jnp.concatenate([key_term, value_term], axis=1))

    query_grad_rot, key_terms = lax.scan(
        grad_step, jnp.zeros((flat_rows, head_dim), jnp.float32), key_blocks
    )
    own_positions = first_row + jnp.arange(local_rows, dtype=jnp.int32)
    keyval_grad = lax.psum_scatter(
        key_terms.reshape(seq_len, 2 * head_dim).astype(jnp.bfloat16),
        "ctx",
        scatter_dimension=0,
        tiled=True,
    ).astype(jnp.float32)
    query_grad = (
        unrotate(query_grad_rot, flat_pos)
        .reshape(local_rows, group * head_dim)
        .astype(jnp.bfloat16)
    )
    query_grad = stored_to_seq(query_grad, block_order, device, ctx_size, per_device)
    key_grad = unrotate(keyval_grad[:, :head_dim], own_positions).astype(jnp.bfloat16)
    value_grad = keyval_grad[:, head_dim:].astype(jnp.bfloat16)
    qkv_grad = jnp.concatenate([query_grad, key_grad, value_grad], axis=1)
    projected = contract_cols(qkv_grad, lax.all_gather(in_weight, "ctx", axis=0, tiled=True))
    section_grad = (section_grad_in.astype(jnp.float32) + projected).astype(jnp.bfloat16)
    passed = passed_along_2(section_grad, "pipe", -1)
    return passed[None]


def solution(mesh):
    return jax.shard_map(
        body,
        mesh=mesh,
        in_specs=(
            P("pipe", "ctx", None),
            P("pipe", "ctx", None),
            P("pipe", "ctx", None),
            P("pipe", "ctx", None),
            P("pipe", "ctx", None),
            P("pipe", None),
            P("pipe", None),
        ),
        out_specs=P("pipe", "ctx", None),
        check_vma=False,
    )
```

profile of v0, /device:TPU:1, one launch (start us, length us, event | category | flops | bytes accessed | tf_op | source)
XLA Modules:
  0.0 424.1 jit_solution(3476864368131219313)
XLA Ops:
  14.5 42.2 %all-gather.7.cloned.1.call-done = bf16[1,4096,256]{2,1,0:T(8,128)(2,1)} async-done(((bf16[1,256,256]{2,1,0:T(8,128)(2,1)}), bf16[1,4096,256]{2,1,0:T(8,128)(2,1)}) %all-gather.7.cloned.1.call-update) | async-done | bytes 2097168 | tf_op jit(solution)/shard_map/all_gather | solution.py:129
  56.7 3.6 gather_fusion
  60.3 51.0 %while.28 = (s32[]{:T(128)}, f32[1024]{0:T(1024)S(1)}, f32[1024]{0:T(1024)S(1)}, f32[1024,128]{1,0:T(8,128)}, s32[8,512]{1,0:T(8,128)S(1)}, /*index=5*/s32[8,512...) while((s32[]{:T(128)}, f32[1024]{0:T(1024)S(1)}, ...), condition=%wide.region_7.8_spmd.clone, body=%wide.region_4.7_spmd.clone.sunk | while | flops 949883904 | bytes 12720321 | solution.py:174
  63.4 2.4 convolution_add_fusion.4
  69.8 2.4 convolution_add_fusion.4
  76.2 2.4 convolution_add_fusion.4
  82.6 2.4 convolution_add_fusion.4
  88.9 2.4 convolution_add_fusion.4
  95.3 2.4 convolution_add_fusion.4
  101.7 2.4 convolution_add_fusion.4
  108.0 2.4 convolution_add_fusion.4
  111.3 18.4 %all-gather.9.cloned.1.call-done = bf16[1,8192,512]{2,1,0:T(8,128)(2,1)} async-done(((bf16[1,512,512]{2,1,0:T(8,128)(2,1)}), bf16[1,8192,512]{2,1,0:T(8,128)(2,1)}) %all-gather.9.cloned.1.call-update) | async-done | bytes 8388624 | tf_op jit(solution)/shard_map/all_gather | solution.py:124
  129.7 7.0 %fusion.43 = bf16[256,512]{1,0:T(8,128)(2,1)S(1)} fusion(bf16[1,8192,512]{2,1,0:T(8,128)(2,1)} %all-gather.9.cloned.1.call-done, bf16[1,256,8192]{2,1,0:T(8,128)(2,1)} %param.11), kind=kOutput, calls=%fused_computation.55 | convolution fusion | flops 2147614720 | bytes 12845056 | tf_op jit(solution)/shard_map/dot_general | solution.py:122
  136.7 2.8 collective-permute-start
  139.5 3.2 collective-permute-done
  143.3 41.0 %while.29 = (s32[]{:T(128)}, f32[1024,128]{1,0:T(8,128)S(1)}, bf16[8,512,256]{2,1,0:T(8,128)(2,1)}, s32[8,512]{1,0:T(8,128)S(1)}, s32[8,512]{1,0:T(8,128)S(1)}, ...) while((s32[]{:T(128)}, f32[1024,128]{1,0:T(8,128)S(1)}, ...), condition=%wide.region_10.11_spmd.clone, body=%wide.region_9.10_spmd.clone.sunk | while | flops 677642240 | bytes 14342807 | solution.py:196
  185.6 2.4 fusion.49
  188.1 2.9 collective-permute-start.1
  191.2 2.4 collective-permute-done.1
  194.6 63.0 %reduce-scatter.2.cloned.1.call-done = bf16[256,256]{1,0:T(8,128)(2,1)} async-done(((bf16[4096,256]{1,0:T(8,128)(2,1)}), bf16[256,256]{1,0:T(8,128)(2,1)}) %reduce-scatter.2.cloned.1.call-update) | async-done | bytes 131088 | tf_op jit(solution)/shard_map/reduce_scatter | solution.py:200
  260.9 89.8 %all-gather.11.cloned.1.call-done = bf16[1,8192,768]{2,1,0:T(8,128)(2,1)} async-done(((bf16[1,512,768]{2,1,0:T(8,128)(2,1)}), bf16[1,8192,768]{2,1,0:T(8,128)(2,1)}) %all-gather.11.cloned.1.call-update) | async-done | bytes 12582928 | tf_op jit(solution)/shard_map/all_gather | solution.py:215
  350.7 14.8 %fusion.37 = bf16[256,8192]{1,0:T(8,128)(2,1)} fusion(bf16[1,8192,768]{2,1,0:T(8,128)(2,1)} %all-gather.11.cloned.1.call-done, bf16[1,256,8192]{2,1,0:T(8,128)(2,1)} %param.11, bf16[256,128]{1,0:T(8,128)(2,1)S(1)} %slice.80, bf16[256,128]{1,0:T(8,128)(2,1)S(1)} %fusion.57, bf16[256,512]{1,0:T(8,128)(2,1)S(1)} %bitcast.123), kind=kOutput, calls=%fused_computation.50 | convolution fusion | flops 3228696576 | bytes 21364736 | tf_op jit(solution)/shard_map/dot_general | solution.py:90
  365.5 2.6 collective-permute-start.2
  368.1 47.5 %collective-permute-done.2 = bf16[256,8192]{1,0:T(8,128)(2,1)S(1)} collective-permute-done((bf16[256,8192]{1,0:T(8,128)(2,1)}, bf16[256,8192]{1,0:T(8,128)(2,1)S(1)}, u32[]{:S(2)}, u32[]{:S(2)}) %collective-permute-start.2) | collective-permute-done | bytes 4194336 | tf_op jit(solution)/shard_map/ppermute | solution.py:21
  (286 shorter events, 86.1 us)
Async XLA Ops:
  6.5 50.2 %all-gather.7.cloned.1.call-start = ((), (), s32[]{:S(2)}) async-start(), calls=%async_computation.2 | async-start | bytes 2228224 | tf_op jit(solution)/shard_map/all_gather | solution.py:129
  7.3 122.5 %all-gather.9.cloned.1.call-start = ((), (), s32[]{:S(2)}) async-start(), calls=%async_computation.3 | async-start | bytes 8912896 | tf_op jit(solution)/shard_map/all_gather | solution.py:124
  8.0 249.6 %reduce-scatter.2.cloned.1.call-start = ((), (), s32[]{:S(2)}) async-start(), calls=%async_computation.1 | async-start | bytes 2228224 | tf_op jit(solution)/shard_map/reduce_scatter | solution.py:200
  62.4 1.0 copy-start
  65.9 0.8 copy-start.1
  68.8 1.1 copy-start
  72.3 0.8 copy-start.1
  75.1 1.1 copy-start
  78.6 0.8 copy-start.1
  81.5 1.0 copy-start
  85.0 0.8 copy-start.1
  87.9 1.0 copy-start
  91.3 0.8 copy-start.1
  94.3 1.0 copy-start
  97.8 0.8 copy-start.1
  100.6 1.0 copy-start
  104.1 0.8 copy-start.1
  107.0 1.0 copy-start
  110.5 0.8 copy-start.1
  111.3 31.6 %copy-start.2 = (f32[1024,128]{1,0:T(8,128)S(1)}, f32[1024,128]{1,0:T(8,128)}, u32[]{:S(2)}) copy-start(f32[1024,128]{1,0:T(8,128)} %get-tuple-element.124) | copy-start | bytes 1572868
  136.7 5.9 %collective-permute-start = (bf16[128,512]{1,0:T(8,128)(2,1)S(1)}, bf16[128,512]{1,0:T(8,128)(2,1)S(1)}, u32[]{:S(2)}, u32[]{:S(2)}) collective-permute-start(bf16[128,512]{1,0:T(8,128)(2,1)S(1)} %get-tuple-element.270), channel_id=1, source_target_pairs={{0,8},{1,9},{2,10},{3,11},{4,12},{5,13},{6,14},{7,15},{8,0},{9,1},... | collective-permute-start | bytes 393224 | tf_op jit(solution)/shard_map/ppermute | solution.py:15
  184.3 166.3 %all-gather.11.cloned.1.call-start = ((), (), s32[]{:S(2)}) async-start(), calls=%async_computation.4 | async-start | bytes 13369344 | tf_op jit(solution)/shard_map/all_gather | solution.py:215
  188.1 5.6 %collective-permute-start.1 = (bf16[128,512]{1,0:T(8,128)(2,1)S(1)}, bf16[128,512]{1,0:T(8,128)(2,1)S(1)}, u32[]{:S(2)}, u32[]{:S(2)}) collective-permute-start(bf16[128,512]{1,0:T(8,128)(2,1)S(1)} %slice.59), channel_id=1, source_target_pairs={{0,8},{1,9},{2,10},{3,11},{4,12},{5,13},{6,14},{7,15},{8,0},{9,1},... | collective-permute-start | bytes 393224 | tf_op jit(solution)/shard_map/ppermute | solution.py:15
  365.5 50.1 %collective-permute-start.2 = (bf16[256,8192]{1,0:T(8,128)(2,1)}, bf16[256,8192]{1,0:T(8,128)(2,1)S(1)}, u32[]{:S(2)}, u32[]{:S(2)}) collective-permute-start(bf16[256,8192]{1,0:T(8,128)(2,1)} %fusion.37), channel_id=1, source_target_pairs={{16,0},{32,16},{48,32},{64,48},{80,64},{96,80},{112,96},{17,1},{33... | collective-permute-start | bytes 12582920 | tf_op jit(solution)/shard_map/ppermute | solution.py:21
Sparse Core Ops, SparseCore 0:
  9.5 47.1 all-gather.6
  58.8 70.8 all-gather.8
  184.4 73.1 reduce-scatter.1
  259.8 90.8 all-gather.10
where the time goes:
time: 425 us; the launch traced here: 424 us
  waiting for transfers between devices  269 us (63%)
  matrix products  68.8 us (16%)
  local copies, waits for them, and re-layouts  49.3 us (12%)
  between operations  14.6 us (3%)
  other arithmetic  13 us (3%)
  starting transfers between devices  8.38 us (2%)
    all_gather x1, waiting for transfers between devices, body(): lax.all_gather(in_weight, 'ctx', axis=0, tiled=True)  89.8 us
    reduce_scatter x1, waiting for transfers between devices, body(): lax.psum_scatter(key_terms.reshape(seq_len, 2 * head_dim).astype(jnp.bflo...  63 us
    ppermute x1, waiting for transfers between devices, passed_along_2(): return lax.ppermute(value, axis, pairs)  47.5 us
    all_gather x1, waiting for transfers between devices, body(): gathered = lax.all_gather(stored_keyval, 'ctx', axis=0, tiled=True)  42.2 us
    dot_general x25, matrix products, contract_cols(): lax.dot_general(left_rows, right_rows, (((1,), (1,)), ((), ())), preferre...  29.2 us
    dot_general x8, matrix products, running_total(): jnp.dot(weights, value_wide, precision=lax.Precision.HIGHEST)  19.4 us
    all_gather x1, waiting for transfers between devices, body(): lax.all_gather(out_weight, 'ctx', axis=0, tiled=True)  18.4 us
    squeeze x16, local copies, waits for them, and re-layouts, body(): lax.scan(running_total, start_carry, key_blocks)  15.7 us
  transfers between devices with their start and end apart: 7, of which 7 were waited for; matrix products, arithmetic and copies ran while one was open for 13% of the time, Pallas kernels for 0%

commit v1 on v0

--- a/solution.py
+++ b/solution.py
@@ -126,7 +126,12 @@
     ).astype(jnp.bfloat16)
     local_out_grad = seq_to_stored(out_grad, block_order, device, ctx_size, per_device)
     query_positions = (block_order[:, None] * BLOCK + within[None, :]).reshape(-1)
-    gathered = lax.all_gather(stored_keyval, "ctx", axis=0, tiled=True)
+    ring = [stored_keyval]
+    for hop in range(15):
+        ring.append(lax.ppermute(ring[-1], "ctx", [(dev, (dev + 1) % 16) for dev in range(16)]))
+    gathered = jnp.roll(
+        jnp.concatenate(ring[::-1], axis=0), (lax.axis_index("ctx") + 1) * ring[0].shape[0], axis=0
+    )
     slot_ids = jnp.arange(block_count, dtype=jnp.int32)
     inverse = jnp.sum(
         jnp.where(block_order[None, :] == slot_ids[:, None], slot_ids[None, :], 0), axis=1

time: 425 us -> 495 us (1.16)
  waiting for transfers between devices: 269 us -> 341 us
  matrix products: 68.8 us -> 80.4 us
  local copies, waits for them, and re-layouts: 49.3 us -> 38.8 us
    ppermute x0 -> x15, waiting for transfers between devices: none -> 110 us  [body(): lax.ppermute(ring[-1], 'ctx', [(dev, (dev + 1) % 16) for dev in range(16)])]
    all_gather x1 -> x0, waiting for transfers between devices: 42.2 us -> none  [body(): gathered = lax.all_gather(stored_keyval, 'ctx', axis=0, tiled=True)]
    reduce_scatter x1, waiting for transfers between devices: 63 us -> 82.2 us  [body(): lax.psum_scatter(key_terms.reshape(seq_len, 2 * head_dim).astype(jnp.bflo...]
    all_gather x1, waiting for transfers between devices: 18.4 us -> 0.01 us  [body(): lax.all_gather(out_weight, 'ctx', axis=0, tiled=True)]
    dot_general x8, matrix products: 19.4 us -> 31.2 us  [running_total(): jnp.dot(weights, value_wide, precision=lax.Precision.HIGHEST)]
    while x40 -> x8, local copies, waits for them, and re-layouts: 9.41 us -> 0.01 us
    ppermute x2, starting transfers between devices: 5.69 us -> 0.39 us  [passed_along(): return lax.ppermute(value, axis, pairs)]
  transfers between devices with their start and end apart: 7 -> 21, of which waited for: 7 -> 20; matrix products, arithmetic and copies ran while one was open for 13% -> 14% of each run, Pallas kernels for 0% -> 0%
where the time goes in v1:
time: 495 us; the launch traced here: 494 us
  waiting for transfers between devices  341 us (69%)
  matrix products  80.4 us (16%)
  local copies, waits for them, and re-layouts  38.8 us (8%)
  between operations  15 us (3%)
  other arithmetic  13 us (3%)
  starting transfers between devices  5.12 us (1%)
    ppermute x15, waiting for transfers between devices, body(): lax.ppermute(ring[-1], 'ctx', [(dev, (dev + 1) % 16) for dev in range(16)])  110 us
    all_gather x1, waiting for transfers between devices, body(): lax.all_gather(in_weight, 'ctx', axis=0, tiled=True)  89.9 us
    reduce_scatter x1, waiting for transfers between devices, body(): lax.psum_scatter(key_terms.reshape(seq_len, 2 * head_dim).astype(jnp.bflo...  82.2 us
    ppermute x1, waiting for transfers between devices, passed_along_2(): return lax.ppermute(value, axis, pairs)  47.5 us
    dot_general x8, matrix products, running_total(): jnp.dot(weights, value_wide, precision=lax.Precision.HIGHEST)  31.2 us
    dot_general x25, matrix products, contract_cols(): lax.dot_general(left_rows, right_rows, (((1,), (1,)), ((), ())), preferre...  29.1 us
    squeeze x16, local copies, waits for them, and re-layouts, body(): lax.scan(running_total, start_carry, key_blocks)  15.6 us
    ppermute x2, waiting for transfers between devices, passed_along(): return lax.ppermute(value, axis, pairs)  10.4 us
  transfers between devices with their start and end apart: 21, of which 20 were waited for; matrix products, arithmetic and copies ran while one was open for 14% of the time, Pallas kernels for 0%

profile of v1, /device:TPU:1, one launch (start us, length us, event | category | flops | bytes accessed | tf_op | source)
XLA Modules:
  0.0 494.3 jit_solution(2750978173943727231)
XLA Ops:
  8.6 7.2 %collective-permute-done = bf16[256,256]{1,0:T(8,128)(2,1)S(1)} collective-permute-done((bf16[256,256]{1,0:T(8,128)(2,1)}, bf16[256,256]{1,0:T(8,128)(2,1)S(1)}, u32[]{:S(2)}, u32[]{:S(2)}) %collective-permute-start) | collective-permute-done | bytes 131104 | tf_op jit(solution)/shard_map/ppermute | solution.py:131
  15.8 7.1 %collective-permute-done.1 = bf16[256,256]{1,0:T(8,128)(2,1)S(1)} collective-permute-done((bf16[256,256]{1,0:T(8,128)(2,1)S(1)}, bf16[256,256]{1,0:T(8,128)(2,1)S(1)}, u32[]{:S(2)}, u32[]{:S(2)}) %collective-permute-start.1) | collective-permute-done | bytes 131104 | tf_op jit(solution)/shard_map/ppermute | solution.py:131
  22.9 7.1 %collective-permute-done.2 = bf16[256,256]{1,0:T(8,128)(2,1)S(1)} collective-permute-done((bf16[256,256]{1,0:T(8,128)(2,1)S(1)}, bf16[256,256]{1,0:T(8,128)(2,1)S(1)}, u32[]{:S(2)}, u32[]{:S(2)}) %collective-permute-start.2) | collective-permute-done | bytes 131104 | tf_op jit(solution)/shard_map/ppermute | solution.py:131
  30.1 7.1 %collective-permute-done.3 = bf16[256,256]{1,0:T(8,128)(2,1)S(1)} collective-permute-done((bf16[256,256]{1,0:T(8,128)(2,1)S(1)}, bf16[256,256]{1,0:T(8,128)(2,1)S(1)}, u32[]{:S(2)}, u32[]{:S(2)}) %collective-permute-start.3) | collective-permute-done | bytes 131104 | tf_op jit(solution)/shard_map/ppermute | solution.py:131
  37.2 7.1 %collective-permute-done.4 = bf16[256,256]{1,0:T(8,128)(2,1)S(1)} collective-permute-done((bf16[256,256]{1,0:T(8,128)(2,1)S(1)}, bf16[256,256]{1,0:T(8,128)(2,1)S(1)}, u32[]{:S(2)}, u32[]{:S(2)}) %collective-permute-start.4) | collective-permute-done | bytes 131104 | tf_op jit(solution)/shard_map/ppermute | solution.py:131
  44.4 7.1 %collective-permute-done.5 = bf16[256,256]{1,0:T(8,128)(2,1)S(1)} collective-permute-done((bf16[256,256]{1,0:T(8,128)(2,1)S(1)}, bf16[256,256]{1,0:T(8,128)(2,1)S(1)}, u32[]{:S(2)}, u32[]{:S(2)}) %collective-permute-start.5) | collective-permute-done | bytes 131104 | tf_op jit(solution)/shard_map/ppermute | solution.py:131
  51.5 7.7 %collective-permute-done.6 = bf16[256,256]{1,0:T(8,128)(2,1)S(1)} collective-permute-done((bf16[256,256]{1,0:T(8,128)(2,1)S(1)}, bf16[256,256]{1,0:T(8,128)(2,1)S(1)}, u32[]{:S(2)}, u32[]{:S(2)}) %collective-permute-start.6) | collective-permute-done | bytes 131104 | tf_op jit(solution)/shard_map/ppermute | solution.py:131
  59.2 8.5 %collective-permute-done.7 = bf16[256,256]{1,0:T(8,128)(2,1)S(1)} collective-permute-done((bf16[256,256]{1,0:T(8,128)(2,1)S(1)}, bf16[256,256]{1,0:T(8,128)(2,1)S(1)}, u32[]{:S(2)}, u32[]{:S(2)}) %collective-permute-start.7) | collective-permute-done | bytes 131104 | tf_op jit(solution)/shard_map/ppermute | solution.py:131
  67.8 7.6 %collective-permute-done.8 = bf16[256,256]{1,0:T(8,128)(2,1)S(1)} collective-permute-done((bf16[256,256]{1,0:T(8,128)(2,1)S(1)}, bf16[256,256]{1,0:T(8,128)(2,1)S(1)}, u32[]{:S(2)}, u32[]{:S(2)}) %collective-permute-start.8) | collective-permute-done | bytes 131104 | tf_op jit(solution)/shard_map/ppermute | solution.py:131
  76.0 6.5 %collective-permute-done.9 = bf16[256,256]{1,0:T(8,128)(2,1)S(1)} collective-permute-done((bf16[256,256]{1,0:T(8,128)(2,1)S(1)}, bf16[256,256]{1,0:T(8,128)(2,1)S(1)}, u32[]{:S(2)}, u32[]{:S(2)}) %collective-permute-start.9) | collective-permute-done | bytes 131104 | tf_op jit(solution)/shard_map/ppermute | solution.py:131
  84.2 5.5 %collective-permute-done.10 = bf16[256,256]{1,0:T(8,128)(2,1)S(1)} collective-permute-done((bf16[256,256]{1,0:T(8,128)(2,1)S(1)}, bf16[256,256]{1,0:T(8,128)(2,1)S(1)}, u32[]{:S(2)}, u32[]{:S(2)}) %collective-permute-start.10) | collective-permute-done | bytes 131104 | tf_op jit(solution)/shard_map/ppermute | solution.py:131
  89.6 9.6 %collective-permute-done.11 = bf16[256,256]{1,0:T(8,128)(2,1)S(1)} collective-permute-done((bf16[256,256]{1,0:T(8,128)(2,1)S(1)}, bf16[256,256]{1,0:T(8,128)(2,1)S(1)}, u32[]{:S(2)}, u32[]{:S(2)}) %collective-permute-start.11) | collective-permute-done | bytes 131104 | tf_op jit(solution)/shard_map/ppermute | solution.py:131
  99.2 8.1 %collective-permute-done.12 = bf16[256,256]{1,0:T(8,128)(2,1)S(1)} collective-permute-done((bf16[256,256]{1,0:T(8,128)(2,1)S(1)}, bf16[256,256]{1,0:T(8,128)(2,1)S(1)}, u32[]{:S(2)}, u32[]{:S(2)}) %collective-permute-start.12) | collective-permute-done | bytes 131104 | tf_op jit(solution)/shard_map/ppermute | solution.py:131
  107.4 7.0 %collective-permute-done.13 = bf16[256,256]{1,0:T(8,128)(2,1)S(1)} collective-permute-done((bf16[256,256]{1,0:T(8,128)(2,1)S(1)}, bf16[256,256]{1,0:T(8,128)(2,1)S(1)}, u32[]{:S(2)}, u32[]{:S(2)}) %collective-permute-start.13) | collective-permute-done | bytes 131104 | tf_op jit(solution)/shard_map/ppermute | solution.py:131
  118.5 6.6 %collective-permute-done.14 = bf16[256,256]{1,0:T(8,128)(2,1)S(1)} collective-permute-done((bf16[256,256]{1,0:T(8,128)(2,1)S(1)}, bf16[256,256]{1,0:T(8,128)(2,1)S(1)}, u32[]{:S(2)}, u32[]{:S(2)}) %collective-permute-start.14) | collective-permute-done | bytes 131104 | tf_op jit(solution)/shard_map/ppermute | solution.py:131
  128.0 53.0 %while.28 = (s32[]{:T(128)}, f32[1024]{0:T(1024)S(1)}, f32[1024]{0:T(1024)S(1)}, f32[1024,128]{1,0:T(8,128)}, s32[8,512]{1,0:T(8,128)S(1)}, /*index=5*/s32[8,512...) while((s32[]{:T(128)}, f32[1024]{0:T(1024)S(1)}, ...), condition=%wide.region_7.8_spmd.clone, body=%wide.region_4.7_spmd.clone.sunk | while | flops 949883904 | bytes 8525961 | solution.py:179
  181.0 7.0 %fusion.43 = bf16[256,512]{1,0:T(8,128)(2,1)S(1)} fusion(bf16[1,8192,512]{2,1,0:T(8,128)(2,1)} %all-gather.5.cloned.1.call-done, bf16[1,256,8192]{2,1,0:T(8,128)(2,1)} %param.11), kind=kOutput, calls=%fused_computation.55 | convolution fusion | flops 2147614720 | bytes 12845056 | tf_op jit(solution)/shard_map/dot_general | solution.py:122
  188.2 5.3 %collective-permute-done.15 = bf16[128,512]{1,0:T(8,128)(2,1)S(1)} collective-permute-done((bf16[128,512]{1,0:T(8,128)(2,1)S(1)}, bf16[128,512]{1,0:T(8,128)(2,1)S(1)}, u32[]{:S(2)}, u32[]{:S(2)}) %collective-permute-start.15) | collective-permute-done | bytes 131104 | tf_op jit(solution)/shard_map/ppermute | solution.py:15
  194.0 40.8 %while.29 = (s32[]{:T(128)}, f32[1024,128]{1,0:T(8,128)S(1)}, bf16[8,512,256]{2,1,0:T(8,128)(2,1)}, s32[8,512]{1,0:T(8,128)S(1)}, s32[8,512]{1,0:T(8,128)S(1)}, ...) while((s32[]{:T(128)}, f32[1024,128]{1,0:T(8,128)S(1)}, ...), condition=%wide.region_10.11_spmd.clone, body=%wide.region_9.10_spmd.clone.sunk | while | flops 677642240 | bytes 14342807 | solution.py:201
  239.3 5.1 %collective-permute-done.16 = bf16[128,512]{1,0:T(8,128)(2,1)S(1)} collective-permute-done((bf16[128,512]{1,0:T(8,128)(2,1)S(1)}, bf16[128,512]{1,0:T(8,128)(2,1)S(1)}, u32[]{:S(2)}, u32[]{:S(2)}) %collective-permute-start.16) | collective-permute-done | bytes 131104 | tf_op jit(solution)/shard_map/ppermute | solution.py:15
  245.4 82.2 %reduce-scatter.2.cloned.1.call-done = bf16[256,256]{1,0:T(8,128)(2,1)} async-done(((bf16[4096,256]{1,0:T(8,128)(2,1)}), bf16[256,256]{1,0:T(8,128)(2,1)}) %reduce-scatter.2.cloned.1.call-update) | async-done | bytes 131088 | tf_op jit(solution)/shard_map/reduce_scatter | solution.py:205
  330.9 89.9 %all-gather.7.cloned.1.call-done = bf16[1,8192,768]{2,1,0:T(8,128)(2,1)} async-done(((bf16[1,512,768]{2,1,0:T(8,128)(2,1)}), bf16[1,8192,768]{2,1,0:T(8,128)(2,1)}) %all-gather.7.cloned.1.call-update) | async-done | bytes 12582928 | tf_op jit(solution)/shard_map/all_gather | solution.py:220
  420.8 14.8 %fusion.37 = bf16[256,8192]{1,0:T(8,128)(2,1)} fusion(bf16[1,8192,768]{2,1,0:T(8,128)(2,1)} %all-gather.7.cloned.1.call-done, bf16[1,256,8192]{2,1,0:T(8,128)(2,1)} %param.11, bf16[256,128]{1,0:T(8,128)(2,1)S(1)} %slice.80, bf16[256,128]{1,0:T(8,128)(2,1)S(1)} %fusion.57, bf16[256,512]{1,0:T(8,128)(2,1)S(1)} %bitcast.127), kind=kOutput, calls=%fused_computation.50 | convolution fusion | flops 3228696576 | bytes 21364736 | tf_op jit(solution)/shard_map/dot_general | solution.py:90
  438.2 47.5 %collective-permute-done.17 = bf16[256,8192]{1,0:T(8,128)(2,1)S(1)} collective-permute-done((bf16[256,8192]{1,0:T(8,128)(2,1)}, bf16[256,8192]{1,0:T(8,128)(2,1)S(1)}, u32[]{:S(2)}, u32[]{:S(2)}) %collective-permute-start.17) | collective-permute-done | bytes 4194336 | tf_op jit(solution)/shard_map/ppermute | solution.py:21
  (316 shorter events, 116.2 us)
Async XLA Ops:
  6.5 118.9 %copy-start.1 = (bf16[1,256,256]{2,1,0:T(8,128)(2,1)S(1)}, bf16[1,256,256]{2,1,0:T(8,128)(2,1)}, u32[]{:S(2)}) copy-start(bf16[1,256,256]{2,1,0:T(8,128)(2,1)} %param.13) | copy-start | bytes 393220
  6.5 174.5 %all-gather.5.cloned.1.call-start = ((), (), s32[]{:S(2)}) async-start(), calls=%async_computation.2 | async-start | bytes 8912896 | tf_op jit(solution)/shard_map/all_gather | solution.py:124
  6.5 9.3 %collective-permute-start = (bf16[256,256]{1,0:T(8,128)(2,1)}, bf16[256,256]{1,0:T(8,128)(2,1)S(1)}, u32[]{:S(2)}, u32[]{:S(2)}) collective-permute-start(bf16[256,256]{1,0:T(8,128)(2,1)} %bitcast.126), channel_id=1, source_target_pairs={{0,1},{1,2},{2,3},{3,4},{4,5},{5,6},{6,7},{7,8},{8,9},{9,10},{10,1... | collective-permute-start | bytes 393224 | tf_op jit(solution)/shard_map/ppermute | solution.py:131
  15.8 7.1 %collective-permute-start.1 = (bf16[256,256]{1,0:T(8,128)(2,1)S(1)}, bf16[256,256]{1,0:T(8,128)(2,1)S(1)}, u32[]{:S(2)}, u32[]{:S(2)}) collective-permute-start(bf16[256,256]{1,0:T(8,128)(2,1)S(1)} %collective-permute-done), channel_id=1, source_target_pairs={{0,1},{1,2},{2,3},{3,4},{4,5},{5,6},{6,7},{7,8},{8,9},{9,10},{10,1... | collective-permute-start | bytes 393224 | tf_op jit(solution)/shard_map/ppermute | solution.py:131
  22.9 7.1 %collective-permute-start.2 = (bf16[256,256]{1,0:T(8,128)(2,1)S(1)}, bf16[256,256]{1,0:T(8,128)(2,1)S(1)}, u32[]{:S(2)}, u32[]{:S(2)}) collective-permute-start(bf16[256,256]{1,0:T(8,128)(2,1)S(1)} %collective-permute-done.1), channel_id=1, source_target_pairs={{0,1},{1,2},{2,3},{3,4},{4,5},{5,6},{6,7},{7,8},{8,9},{9,10},{10,1... | collective-permute-start | bytes 393224 | tf_op jit(solution)/shard_map/ppermute | solution.py:131
  30.1 7.1 %collective-permute-start.3 = (bf16[256,256]{1,0:T(8,128)(2,1)S(1)}, bf16[256,256]{1,0:T(8,128)(2,1)S(1)}, u32[]{:S(2)}, u32[]{:S(2)}) collective-permute-start(bf16[256,256]{1,0:T(8,128)(2,1)S(1)} %collective-permute-done.2), channel_id=1, source_target_pairs={{0,1},{1,2},{2,3},{3,4},{4,5},{5,6},{6,7},{7,8},{8,9},{9,10},{10,1... | collective-permute-start | bytes 393224 | tf_op jit(solution)/shard_map/ppermute | solution.py:131
  37.2 7.1 %collective-permute-start.4 = (bf16[256,256]{1,0:T(8,128)(2,1)S(1)}, bf16[256,256]{1,0:T(8,128)(2,1)S(1)}, u32[]{:S(2)}, u32[]{:S(2)}) collective-permute-start(bf16[256,256]{1,0:T(8,128)(2,1)S(1)} %collective-permute-done.3), channel_id=1, source_target_pairs={{0,1},{1,2},{2,3},{3,4},{4,5},{5,6},{6,7},{7,8},{8,9},{9,10},{10,1... | collective-permute-start | bytes 393224 | tf_op jit(solution)/shard_map/ppermute | solution.py:131
  44.4 7.1 %collective-permute-start.5 = (bf16[256,256]{1,0:T(8,128)(2,1)S(1)}, bf16[256,256]{1,0:T(8,128)(2,1)S(1)}, u32[]{:S(2)}, u32[]{:S(2)}) collective-permute-start(bf16[256,256]{1,0:T(8,128)(2,1)S(1)} %collective-permute-done.4), channel_id=1, source_target_pairs={{0,1},{1,2},{2,3},{3,4},{4,5},{5,6},{6,7},{7,8},{8,9},{9,10},{10,1... | collective-permute-start | bytes 393224 | tf_op jit(solution)/shard_map/ppermute | solution.py:131
  51.5 7.7 %collective-permute-start.6 = (bf16[256,256]{1,0:T(8,128)(2,1)S(1)}, bf16[256,256]{1,0:T(8,128)(2,1)S(1)}, u32[]{:S(2)}, u32[]{:S(2)}) collective-permute-start(bf16[256,256]{1,0:T(8,128)(2,1)S(1)} %collective-permute-done.5), channel_id=1, source_target_pairs={{0,1},{1,2},{2,3},{3,4},{4,5},{5,6},{6,7},{7,8},{8,9},{9,10},{10,1... | collective-permute-start | bytes 393224 | tf_op jit(solution)/shard_map/ppermute | solution.py:131
  59.2 8.5 %collective-permute-start.7 = (bf16[256,256]{1,0:T(8,128)(2,1)S(1)}, bf16[256,256]{1,0:T(8,128)(2,1)S(1)}, u32[]{:S(2)}, u32[]{:S(2)}) collective-permute-start(bf16[256,256]{1,0:T(8,128)(2,1)S(1)} %collective-permute-done.6), channel_id=1, source_target_pairs={{0,1},{1,2},{2,3},{3,4},{4,5},{5,6},{6,7},{7,8},{8,9},{9,10},{10,1... | collective-permute-start | bytes 393224 | tf_op jit(solution)/shard_map/ppermute | solution.py:131
  67.7 7.6 %collective-permute-start.8 = (bf16[256,256]{1,0:T(8,128)(2,1)S(1)}, bf16[256,256]{1,0:T(8,128)(2,1)S(1)}, u32[]{:S(2)}, u32[]{:S(2)}) collective-permute-start(bf16[256,256]{1,0:T(8,128)(2,1)S(1)} %collective-permute-done.7), channel_id=1, source_target_pairs={{0,1},{1,2},{2,3},{3,4},{4,5},{5,6},{6,7},{7,8},{8,9},{9,10},{10,1... | collective-permute-start | bytes 393224 | tf_op jit(solution)/shard_map/ppermute | solution.py:131
  67.7 259.8 %reduce-scatter.2.cloned.1.call-start = ((), (), s32[]{:S(2)}) async-start(), calls=%async_computation.1 | async-start | bytes 2228224 | tf_op jit(solution)/shard_map/reduce_scatter | solution.py:205
  75.3 7.1 %collective-permute-start.9 = (bf16[256,256]{1,0:T(8,128)(2,1)S(1)}, bf16[256,256]{1,0:T(8,128)(2,1)S(1)}, u32[]{:S(2)}, u32[]{:S(2)}) collective-permute-start(bf16[256,256]{1,0:T(8,128)(2,1)S(1)} %collective-permute-done.8), channel_id=1, source_target_pairs={{0,1},{1,2},{2,3},{3,4},{4,5},{5,6},{6,7},{7,8},{8,9},{9,10},{10,1... | collective-permute-start | bytes 393224 | tf_op jit(solution)/shard_map/ppermute | solution.py:131
  82.5 7.1 %collective-permute-start.10 = (bf16[256,256]{1,0:T(8,128)(2,1)S(1)}, bf16[256,256]{1,0:T(8,128)(2,1)S(1)}, u32[]{:S(2)}, u32[]{:S(2)}) collective-permute-start(bf16[256,256]{1,0:T(8,128)(2,1)S(1)} %collective-permute-done.9), channel_id=1, source_target_pairs={{0,1},{1,2},{2,3},{3,4},{4,5},{5,6},{6,7},{7,8},{8,9},{9,10},{10,1... | collective-permute-start | bytes 393224 | tf_op jit(solution)/shard_map/ppermute | solution.py:131
  89.6 9.6 %collective-permute-start.11 = (bf16[256,256]{1,0:T(8,128)(2,1)S(1)}, bf16[256,256]{1,0:T(8,128)(2,1)S(1)}, u32[]{:S(2)}, u32[]{:S(2)}) collective-permute-start(bf16[256,256]{1,0:T(8,128)(2,1)S(1)} %collective-permute-done.10), channel_id=1, source_target_pairs={{0,1},{1,2},{2,3},{3,4},{4,5},{5,6},{6,7},{7,8},{8,9},{9,10},{10,1... | collective-permute-start | bytes 393224 | tf_op jit(solution)/shard_map/ppermute | solution.py:131
  99.2 8.1 %collective-permute-start.12 = (bf16[256,256]{1,0:T(8,128)(2,1)S(1)}, bf16[256,256]{1,0:T(8,128)(2,1)S(1)}, u32[]{:S(2)}, u32[]{:S(2)}) collective-permute-start(bf16[256,256]{1,0:T(8,128)(2,1)S(1)} %collective-permute-done.11), channel_id=1, source_target_pairs={{0,1},{1,2},{2,3},{3,4},{4,5},{5,6},{6,7},{7,8},{8,9},{9,10},{10,1... | collective-permute-start | bytes 393224 | tf_op jit(solution)/shard_map/ppermute | solution.py:131
  107.3 7.1 %collective-permute-start.13 = (bf16[256,256]{1,0:T(8,128)(2,1)S(1)}, bf16[256,256]{1,0:T(8,128)(2,1)S(1)}, u32[]{:S(2)}, u32[]{:S(2)}) collective-permute-start(bf16[256,256]{1,0:T(8,128)(2,1)S(1)} %collective-permute-done.12), channel_id=1, source_target_pairs={{0,1},{1,2},{2,3},{3,4},{4,5},{5,6},{6,7},{7,8},{8,9},{9,10},{10,1... | collective-permute-start | bytes 393224 | tf_op jit(solution)/shard_map/ppermute | solution.py:131
  114.4 10.7 %collective-permute-start.14 = (bf16[256,256]{1,0:T(8,128)(2,1)S(1)}, bf16[256,256]{1,0:T(8,128)(2,1)S(1)}, u32[]{:S(2)}, u32[]{:S(2)}) collective-permute-start(bf16[256,256]{1,0:T(8,128)(2,1)S(1)} %collective-permute-done.13), channel_id=1, source_target_pairs={{0,1},{1,2},{2,3},{3,4},{4,5},{5,6},{6,7},{7,8},{8,9},{9,10},{10,1... | collective-permute-start | bytes 393224 | tf_op jit(solution)/shard_map/ppermute | solution.py:131
  181.0 12.7 %copy-start = (f32[1024,128]{1,0:T(8,128)S(1)}, f32[1024,128]{1,0:T(8,128)}, u32[]{:S(2)}) copy-start(f32[1024,128]{1,0:T(8,128)} %get-tuple-element.124) | copy-start | bytes 1572868
  188.1 5.4 %collective-permute-start.15 = (bf16[128,512]{1,0:T(8,128)(2,1)S(1)}, bf16[128,512]{1,0:T(8,128)(2,1)S(1)}, u32[]{:S(2)}, u32[]{:S(2)}) collective-permute-start(bf16[128,512]{1,0:T(8,128)(2,1)S(1)} %get-tuple-element.270), channel_id=1, source_target_pairs={{0,8},{1,9},{2,10},{3,11},{4,12},{5,13},{6,14},{7,15},{8,0},{9,1},... | collective-permute-start | bytes 393224 | tf_op jit(solution)/shard_map/ppermute | solution.py:15
  234.9 185.9 %all-gather.7.cloned.1.call-start = ((), (), s32[]{:S(2)}) async-start(), calls=%async_computation.3 | async-start | bytes 13369344 | tf_op jit(solution)/shard_map/all_gather | solution.py:220
  238.8 5.6 %collective-permute-start.16 = (bf16[128,512]{1,0:T(8,128)(2,1)S(1)}, bf16[128,512]{1,0:T(8,128)(2,1)S(1)}, u32[]{:S(2)}, u32[]{:S(2)}) collective-permute-start(bf16[128,512]{1,0:T(8,128)(2,1)S(1)} %slice.59), channel_id=1, source_target_pairs={{0,8},{1,9},{2,10},{3,11},{4,12},{5,13},{6,14},{7,15},{8,0},{9,1},... | collective-permute-start | bytes 393224 | tf_op jit(solution)/shard_map/ppermute | solution.py:15
  435.6 50.1 %collective-permute-start.17 = (bf16[256,8192]{1,0:T(8,128)(2,1)}, bf16[256,8192]{1,0:T(8,128)(2,1)S(1)}, u32[]{:S(2)}, u32[]{:S(2)}) collective-permute-start(bf16[256,8192]{1,0:T(8,128)(2,1)} %fusion.37), channel_id=1, source_target_pairs={{16,0},{32,16},{48,32},{64,48},{80,64},{96,80},{112,96},{17,1},{33... | collective-permute-start | bytes 12582920 | tf_op jit(solution)/shard_map/ppermute | solution.py:21
Sparse Core Ops, SparseCore 0:
  67.9 88.5 all-gather.4
  235.0 92.5 reduce-scatter.1
  329.9 90.8 all-gather.6
